TPU v7x, 128 devices: a whole 4x4x4 slice. The times are simulated.
128 devices in a mesh: row: 8 (over x, core), col: 16 (over z, y).
Axes of the slice: x: 4, y: 4, z: 4, core: 2. Of those that a mesh axis runs over, the one named last changes fastest.
Arguments:
- left_factor: float32 [23, 8, 128, 16, 16, 128], P(None, 'row', None, None, 'col'), may hold values from -5 to 5
- pick_site: int32 [23, 8, 128], P(None, 'row'), may hold values from 0 to 131071
- noise: float32 [23, 8, 128], P(None, 'row'), may hold values from 2 to 5
Outputs:
- panels: float32 [8, 16, 184, 2, 128], P('row', 'col')
All inputs are finite; a program needn't handle non-finite values.
Results may differ from a plain program's by a relative error of at most 0.000064.
Values sent between devices are 32-bit elements; how exact they have to be, the bound alone decides.
No kernel may reach another device: no remote copies, remote signals or barrier semaphores. Data moves between devices by JAX's collectives and lax.ppermute only.
A program may use at most 128 MiB of HBM per device.

v0:
```python
import jax
import jax.numpy as jnp
from jax import lax
from jax.sharding import PartitionSpec as P

GRID_Y = 64
GRID_Z = 32


LATERAL = 24.0
VERTICAL = 6.0


def site_coords(site_ids):
    coord_x = site_ids // (GRID_Y * GRID_Z)
    coord_y = site_ids // GRID_Z % GRID_Y
    coord_z = site_ids % GRID_Z
    return jnp.stack([coord_x, coord_y, coord_z]).astype(jnp.float32)


def matern(row_coords, col_coords):
    lengths = (LATERAL, LATERAL, VERTICAL)
    squared = jnp.zeros((row_coords.shape[1], col_coords.shape[1]), jnp.float32)
    for dim_index in range(3):
        difference = (row_coords[dim_index][:, None] - col_coords[dim_index][None, :]) / lengths[
            dim_index
        ]
        squared = squared + difference * difference
    radius = jnp.sqrt(3.0 * squared)
    return (1.0 + radius) * jnp.exp(-radius)


def times_transposed(left_mat, right_mat, precision=lax.Precision.HIGHEST):
    return lax.dot_general(
        left_mat,
        right_mat,
        (((1,), (1,)), ((), ())),
        precision=precision,
        preferred_element_type=jnp.float32,
    )


def lower_inverse(square):
    factor = jnp.linalg.cholesky(square)
    return jax.scipy.linalg.solve_triangular(
        factor, jnp.eye(square.shape[0], dtype=jnp.float32), lower=True
    )


def col_sum(block):
    count = lax.axis_size("col")
    group = 1
    while group < count:
        width = min(4, count // group)
        parts = [
            lax.ppermute(block, "col", [(i, i ^ (k * group)) for i in range(count)])
            for k in range(1, width)
        ]
        for part in parts:
            block = block + part
        group *= width
    return block


def row_broadcast(pack):
    row = lax.axis_index("row")
    swap_home = lax.ppermute(pack, "row", [(0, 1), (1, 0)])
    first_out = lax.ppermute(pack, "row", [(0, 2), (1, 7)])
    relay = lax.ppermute(first_out, "row", [(2, 4), (7, 5)])
    second_out = lax.ppermute(
        jnp.where(row < 2, pack, first_out), "row", [(1, 3), (0, 6)]
    )
    hand = jnp.where(
        row < 2,
        pack,
        jnp.where((row == 2) | (row == 7), first_out, jnp.where((row == 4) | (row == 5), relay, second_out)),
    )
    swap_far = lax.ppermute(hand, "row", [(2, 3), (3, 2), (4, 5), (5, 4), (6, 7), (7, 6)])
    other = jnp.where(row < 2, swap_home, swap_far)
    return hand, other


def col_scatter(blocks):
    count = lax.axis_size("col")
    me = lax.axis_index("col")
    ring = 4
    order = [0, 3, 1, 2]
    shaped = blocks.reshape((ring, ring) + blocks.shape[1:])
    shaped = jnp.stack([shaped[z] for z in order])
    shaped = jnp.stack([shaped[:, y] for y in order], axis=1)
    shaped = shaped.reshape((2, 2, 2, 2) + blocks.shape[1:])
    my_z, my_y = me // ring, me % ring

    def pairs(step_of):
        return [(z * ring + y, step_of(z, y)) for z in range(ring) for y in range(ring)]

    steps = (
        (2, (my_y ^ (my_y >> 1)) % 2, pairs(lambda z, y: z * ring + (y ^ 1))),
        (0, (my_z ^ (my_z >> 1)) % 2, pairs(lambda z, y: (z ^ 1) * ring + y)),
        (1, my_y >> 1, pairs(lambda z, y: z * ring + (ring - 1 - y))),
        (0, my_z >> 1, pairs(lambda z, y: (ring - 1 - z) * ring + y)),
    )
    for axis, mine, perm in steps:
        keep = lax.dynamic_index_in_dim(shaped, mine, axis, keepdims=False)
        send = lax.dynamic_index_in_dim(shaped, 1 - mine, axis, keepdims=False)
        shaped = keep + lax.ppermute(send, "col", perm)
    return shaped


def body(left_factor, pick_site, noise):
    row_blocks, _, block_width, col_blocks, _, _ = left_factor.shape
    col_count = lax.axis_size("col")
    row_share = row_blocks * block_width // col_count
    row_index = lax.axis_index("row")
    col_index = lax.axis_index("col")
    local_rows = left_factor.reshape(row_blocks * block_width, col_blocks * block_width)
    site_flat = pick_site.reshape(row_blocks * block_width)
    noise_flat = noise.reshape(row_blocks * block_width)
    offset = col_index * row_share
    my_coords = site_coords(lax.dynamic_slice_in_dim(site_flat, offset, row_share))
    my_noise = lax.dynamic_slice_in_dim(noise_flat, offset, row_share)
    first_owner = (row_index == 0) & (col_index == 0)
    second_owner = (row_index == 1) & (col_index == 0)
    own_diag = jnp.diag(my_noise[:block_width])

    head_rows = local_rows[:block_width]
    head_info = jnp.concatenate(
        [site_coords(site_flat[:block_width]), noise_flat[None, :block_width]], axis=0
    )
    is_first = row_index == 0
    is_second = row_index == 1
    info_rows = jnp.zeros((8, head_rows.shape[1]), jnp.float32).at[:4, :block_width].set(head_info)
    hand, other = row_broadcast(jnp.concatenate([head_rows, info_rows], axis=0))
    is_even = row_index % 2 == 0
    first_pack = jnp.where(is_even, hand, other)
    second_pack = jnp.where(is_even, other, hand)
    heads = jnp.concatenate([first_pack[:block_width], second_pack[:block_width]], axis=0)
    info = jnp.concatenate(
        [first_pack[block_width : block_width + 4, :block_width],
         second_pack[block_width : block_width + 4, :block_width]],
        axis=1,
    )

    gram_11 = col_sum(times_transposed(heads[:block_width], heads[:block_width]))
    gram_2x = col_sum(times_transposed(heads[block_width:], heads))
    gram_21 = gram_2x[:, :block_width]
    gram_22 = gram_2x[:, block_width:]
    terms = times_transposed(local_rows, heads, lax.Precision.HIGH).reshape(
        col_count, row_share, 2 * block_width
    )
    sums = col_scatter(terms)

    first_coords = info[:3, :block_width]
    second_coords = info[:3, block_width:]
    first_diag = matern(first_coords, first_coords) - gram_11
    first_diag = first_diag + jnp.diag(info[3, :block_width])
    first_inverse = lower_inverse(first_diag)
    cross_rows = times_transposed(
        matern(second_coords, first_coords) - gram_21, first_inverse
    )
    second_diag = (
        matern(second_coords, second_coords)
        - gram_22
        - times_transposed(cross_rows, cross_rows)
    )
    second_diag = second_diag + jnp.diag(info[3, block_width:])
    second_inverse = lower_inverse(second_diag)

    first_cov = matern(my_coords, first_coords) - sums[:, :block_width]
    first_cov = first_cov.at[:block_width].add(jnp.where(first_owner, own_diag, 0.0))
    first_panel = times_transposed(first_cov, first_inverse)
    second_cov = (
        (matern(my_coords, second_coords) - sums[:, block_width:])
        - times_transposed(first_panel, cross_rows)
    )
    second_cov = second_cov.at[:block_width].add(jnp.where(second_owner, own_diag, 0.0))
    second_panel = times_transposed(second_cov, second_inverse)
    stacked = jnp.stack([first_panel, second_panel], axis=1)
    return stacked.reshape(1, 1, row_share, 2, block_width)


def solution(mesh):
    placed = (P(None, "row", None, None, "col", None), P(None, "row", None), P(None, "row", None))
    return jax.shard_map(
        body,
        mesh=mesh,
        in_specs=placed,
        out_specs=P("row", "col", None, None, None),
        check_vma=False,
    )
```

profile of v0, /device:TPU:4, one launch (start us, length us, event | category | flops | bytes accessed | tf_op | source)
XLA Modules:
  0.0 178.9 jit_solution(1856049228524799051)
XLA Ops:
  1.3 4.0 %slice_reduce_fusion = f32[128,16,128]{2,1,0:T(8,128)S(1)} fusion(f32[23,1,128,16,1,128]{5,4,3,2,1,0:T(1,128)} %param.12), kind=kLoop, calls=%fused_computation.28 | loop fusion | bytes 2097152 | tf_op jit(solution)/shard_map/slice | solution.py:126
  8.8 1.3 collective-permute-start.1
  10.1 1.7 collective-permute-start.3
  12.8 27.8 %collective-permute-done.1 = f32[136,2048]{1,0:T(8,128)} collective-permute-done((f32[136,2048]{1,0:T(8,128)S(1)}, f32[136,2048]{1,0:T(8,128)}, u32[]{:S(2)}, u32[]{:S(2)}) %collective-permute-start.1) | collective-permute-done | bytes 1114144 | tf_op jit(solution)/shard_map/ppermute | solution.py:69
  40.6 1.6 select_select_fusion
  42.2 1.9 %collective-permute-start.4 = (f32[136,2048]{1,0:T(8,128)S(1)}, f32[136,2048]{1,0:T(8,128)S(1)}, u32[]{:S(2)}, u32[]{:S(2)}) collective-permute-start(f32[136,2048]{1,0:T(8,128)S(1)} %select_select_fusion), channel_id=1, source_target_pairs={{32,48},{48,32},{64,80},{80,64},{96,112},{112,96},{33,49},{49,33},... | collective-permute-start | bytes 3342344 | tf_op jit(solution)/shard_map/ppermute | solution.py:78
  47.2 1.8 %fusion.9 = f32[128,256]{0,1:T(8,128)S(1)} fusion(f32[128,2048]{1,0:T(8,128)S(1)} %slice.246, f32[128,2048]{1,0:T(8,128)S(1)} %slice.245), kind=kOutput, calls=%fused_computation.21 | convolution fusion | flops 805830656 | bytes 2228224 | tf_op jit(solution)/shard_map/dot_general | solution.py:34
  49.0 1.7 collective-permute-start.15
  50.6 2.9 %collective-permute-start.16 = (f32[128,256]{0,1:T(8,128)S(1)}, f32[128,256]{0,1:T(8,128)}, u32[]{:S(2)}, u32[]{:S(2)}) collective-permute-start(f32[128,256]{0,1:T(8,128)S(1)} %fusion.9), channel_id=1, source_target_pairs={{0,2},{1,3},{2,0},{3,1},{4,6},{5,7},{6,4},{7,5},{8,10},{9,11},{10,... | collective-permute-start | bytes 393224 | tf_op jit(solution)/shard_map/ppermute | solution.py:56
  55.3 2.2 %collective-permute-start.11 = (f32[128,128]{0,1:T(8,128)S(1)}, f32[128,128]{0,1:T(8,128)}, u32[]{:S(2)}, u32[]{:S(2)}) collective-permute-start(f32[128,128]{0,1:T(8,128)S(1)} %fusion.64), channel_id=1, source_target_pairs={{0,3},{1,2},{2,1},{3,0},{4,7},{5,6},{6,5},{7,4},{8,11},{9,10},{10,... | collective-permute-start | bytes 196616 | tf_op jit(solution)/shard_map/ppermute | solution.py:56
  58.7 26.0 %fusion.3 = f32[2944,256]{0,1:T(8,128)S(1)} fusion(f32[368,8,16,128]{3,2,1,0:T(8,128)} %bitcast.117, f32[128,2048]{1,0:T(8,128)S(1)} %slice.246, f32[128,2048]{1,0:T(8,128)S(1)} %slice.245), kind=kOutput, calls=%fused_computation.5 | convolution fusion | flops 9261547520 | bytes 29229056 | tf_op jit(solution)/shard_map/dot_general | solution.py:34
  85.4 1.1 copy.37
  86.6 1.1 copy.38
  87.7 1.2 copy.39
  88.9 1.1 copy.40
  90.0 3.2 %fusion.6 = f32[4,4,184,256]{3,2,1,0:T(8,128)S(1)} fusion(f32[1,4,184,256]{3,2,1,0:T(8,128)} %bitcast.127, f32[1,4,184,256]{3,2,1,0:T(8,128)} %bitcast.126, f32[1,4,184,256]{3,2,1,0:T(8,128)} %bitcast.125, f32[1,4,184,256]{3,2,1,0:T(8,128)} %bitcast.124), kind=kLoop, calls=%fused_computation.7 | loop fusion | flops 21102592 | bytes 6029312 | tf_op jit(solution)/shard_map/stack | solution.py:90
  93.2 1.3 dynamic-slice_bitcast_fusion
  95.1 1.2 collective-permute-start.5
  97.2 2.0 %collective-permute-start.12 = (f32[128,128]{0,1:T(8,128)S(1)}, f32[128,128]{0,1:T(8,128)S(1)}, u32[]{:S(2)}, u32[]{:S(2)}) collective-permute-start(f32[128,128]{0,1:T(8,128)S(1)} %add_add_fusion.2), channel_id=1, source_target_pairs={{0,4},{1,5},{2,6},{3,7},{4,0},{5,1},{6,2},{7,3},{8,12},{9,13},{10,... | collective-permute-start | bytes 196616 | tf_op jit(solution)/shard_map/ppermute | solution.py:56
  99.2 3.6 %collective-permute-start.13 = (f32[128,128]{0,1:T(8,128)S(1)}, f32[128,128]{0,1:T(8,128)S(1)}, u32[]{:S(2)}, u32[]{:S(2)}) collective-permute-start(f32[128,128]{0,1:T(8,128)S(1)} %add_add_fusion.2), channel_id=1, source_target_pairs={{0,8},{1,9},{2,10},{3,11},{4,12},{5,13},{6,14},{7,15},{8,0},{9,1},... | collective-permute-start | bytes 196616 | tf_op jit(solution)/shard_map/ppermute | solution.py:56
  103.9 4.7 %collective-permute-start.19 = (f32[128,256]{0,1:T(8,128)S(1)}, f32[128,256]{0,1:T(8,128)S(1)}, u32[]{:S(2)}, u32[]{:S(2)}) collective-permute-start(f32[128,256]{0,1:T(8,128)S(1)} %add_add_fusion.1), channel_id=1, source_target_pairs={{0,8},{1,9},{2,10},{3,11},{4,12},{5,13},{6,14},{7,15},{8,0},{9,1},... | collective-permute-start | bytes 393224 | tf_op jit(solution)/shard_map/ppermute | solution.py:56
  108.6 1.5 collective-permute-done.14
  111.0 12.5 %cholesky.44 = f32[128,128]{1,0:T(8,128)S(1)} custom-call(f32[128,128]{1,0:T(8,128)} %fusion.27), custom_call_target="Cholesky" | custom-call | tf_op jit(solution)/shard_map/jit(cholesky)/cholesky | solution.py:44
  124.9 10.4 %custom-call.6 = f32[1,128,128]{1,2,0:T(8,128)} custom-call(f32[1,128,128]{2,1,0:T(8,128)S(1)} %fusion.15), custom_call_target="InvertDiagBlocksLowerTriangular" | custom-call | tf_op jit(solution)/shard_map/jit(_solve_triangular)/triangular_solve | solution.py:45
  136.5 1.6 bitcast_add_fusion
  138.1 1.1 copy-done
  141.2 11.7 %cholesky.55 = f32[128,128]{1,0:T(8,128)S(1)} custom-call(f32[128,128]{1,0:T(8,128)S(1)} %fusion.25), custom_call_target="Cholesky" | custom-call | tf_op jit(solution)/shard_map/jit(cholesky)/cholesky | solution.py:44
  153.4 1.2 bitcast_add_fusion.1
  154.9 2.5 %collective-permute-start.7 = (f32[2,184,256]{1,2,0:T(8,128)S(1)}, f32[2,184,256]{1,2,0:T(8,128)S(1)}, u32[]{:S(2)}, u32[]{:S(2)}) collective-permute-start(f32[2,184,256]{1,2,0:T(8,128)S(1)} %bitcast.128), channel_id=1, source_target_pairs={{0,3},{1,2},{2,1},{3,0},{4,7},{5,6},{6,5},{7,4},{8,11},{9,10},{10,... | collective-permute-start | bytes 1130504 | tf_op jit(solution)/shard_map/ppermute | solution.py:106
  158.8 9.8 %custom-call.7 = f32[1,128,128]{1,2,0:T(8,128)S(1)} custom-call(f32[1,128,128]{2,1,0:T(8,128)S(1)} %fusion.16), custom_call_target="InvertDiagBlocksLowerTriangular" | custom-call | tf_op jit(solution)/shard_map/jit(_solve_triangular)/triangular_solve | solution.py:45
  168.9 3.0 %collective-permute-start.8 = (f32[184,256]{0,1:T(8,128)S(1)}, f32[184,256]{0,1:T(8,128)S(1)}, u32[]{:S(2)}, u32[]{:S(2)}) collective-permute-start(f32[184,256]{0,1:T(8,128)S(1)} %dynamic-slice_bitcast_fusion.2), channel_id=1, source_target_pairs={{0,12},{1,13},{2,14},{3,15},{4,8},{5,9},{6,10},{7,11},{8,4},{9,5},... | collective-permute-start | bytes 565256 | tf_op jit(solution)/shard_map/ppermute | solution.py:106
  172.2 4.4 %collective-permute-done.8 = f32[184,256]{0,1:T(8,128)S(1)} collective-permute-done((f32[184,256]{0,1:T(8,128)S(1)}, f32[184,256]{0,1:T(8,128)S(1)}, u32[]{:S(2)}, u32[]{:S(2)}) %collective-permute-start.8) | collective-permute-done | bytes 188448 | tf_op jit(solution)/shard_map/ppermute | solution.py:106
  (105 shorter events, 25.1 us)
Async XLA Ops:
  5.8 0.8 collective-permute-start
  7.9 36.2 %copy-start.3 = (s32[23,1,128]{2,1,0:T(1,128)S(1)}, s32[23,1,128]{2,1,0:T(1,128)}, u32[]{:S(2)}) copy-start(s32[23,1,128]{2,1,0:T(1,128)} %param.13) | copy-start | bytes 35332
  7.9 36.3 %copy-start.4 = (f32[23,1,128]{2,1,0:T(1,128)S(1)}, f32[23,1,128]{2,1,0:T(1,128)}, u32[]{:S(2)}) copy-start(f32[23,1,128]{2,1,0:T(1,128)} %param.14) | copy-start | bytes 35332
  7.9 3.8 %collective-permute-start.2 = (f32[136,2048]{1,0:T(8,128)}, f32[136,2048]{1,0:T(8,128)S(1)}, u32[]{:S(2)}, u32[]{:S(2)}) collective-permute-start(f32[136,2048]{1,0:T(8,128)} %broadcast_select_fusion.1), channel_id=1, source_target_pairs={{16,48},{0,96},{17,49},{1,97},{18,50},{2,98},{19,51},{3,99},{20,52... | collective-permute-start | bytes 3342344 | tf_op jit(solution)/shard_map/ppermute | solution.py:70
  8.8 31.8 %collective-permute-start.1 = (f32[136,2048]{1,0:T(8,128)S(1)}, f32[136,2048]{1,0:T(8,128)}, u32[]{:S(2)}, u32[]{:S(2)}) collective-permute-start(f32[136,2048]{1,0:T(8,128)S(1)} %collective-permute-done), channel_id=1, source_target_pairs={{32,64},{112,80},{33,65},{113,81},{34,66},{114,82},{35,67},{115,83... | collective-permute-start | bytes 3342344 | tf_op jit(solution)/shard_map/ppermute | solution.py:69
  10.1 35.6 %collective-permute-start.3 = (f32[136,2048]{1,0:T(8,128)}, f32[136,2048]{1,0:T(8,128)}, u32[]{:S(2)}, u32[]{:S(2)}) collective-permute-start(f32[136,2048]{1,0:T(8,128)} %copy-done.2), channel_id=1, source_target_pairs={{0,16},{16,0},{1,17},{17,1},{2,18},{18,2},{3,19},{19,3},{4,20},{20... | collective-permute-start | bytes 3342344 | tf_op jit(solution)/shard_map/ppermute | solution.py:67
  42.2 4.6 %collective-permute-start.4 = (f32[136,2048]{1,0:T(8,128)S(1)}, f32[136,2048]{1,0:T(8,128)S(1)}, u32[]{:S(2)}, u32[]{:S(2)}) collective-permute-start(f32[136,2048]{1,0:T(8,128)S(1)} %select_select_fusion), channel_id=1, source_target_pairs={{32,48},{48,32},{64,80},{80,64},{96,112},{112,96},{33,49},{49,33},... | collective-permute-start | bytes 3342344 | tf_op jit(solution)/shard_map/ppermute | solution.py:78
  49.0 50.2 %collective-permute-start.15 = (f32[128,256]{0,1:T(8,128)S(1)}, f32[128,256]{0,1:T(8,128)S(1)}, u32[]{:S(2)}, u32[]{:S(2)}) collective-permute-start(f32[128,256]{0,1:T(8,128)S(1)} %fusion.9), channel_id=1, source_target_pairs={{0,1},{1,0},{2,3},{3,2},{4,5},{5,4},{6,7},{7,6},{8,9},{9,8},{10,11... | collective-permute-start | bytes 393224 | tf_op jit(solution)/shard_map/ppermute | solution.py:56
  50.6 52.2 %collective-permute-start.16 = (f32[128,256]{0,1:T(8,128)S(1)}, f32[128,256]{0,1:T(8,128)}, u32[]{:S(2)}, u32[]{:S(2)}) collective-permute-start(f32[128,256]{0,1:T(8,128)S(1)} %fusion.9), channel_id=1, source_target_pairs={{0,2},{1,3},{2,0},{3,1},{4,6},{5,7},{6,4},{7,5},{8,10},{9,11},{10,... | collective-permute-start | bytes 393224 | tf_op jit(solution)/shard_map/ppermute | solution.py:56
  54.5 40.0 %collective-permute-start.10 = (f32[128,128]{0,1:T(8,128)S(1)}, f32[128,128]{0,1:T(8,128)S(1)}, u32[]{:S(2)}, u32[]{:S(2)}) collective-permute-start(f32[128,128]{0,1:T(8,128)S(1)} %fusion.64), channel_id=1, source_target_pairs={{0,2},{1,3},{2,0},{3,1},{4,6},{5,7},{6,4},{7,5},{8,10},{9,11},{10,... | collective-permute-start | bytes 196616 | tf_op jit(solution)/shard_map/ppermute | solution.py:56
  55.3 39.9 %collective-permute-start.11 = (f32[128,128]{0,1:T(8,128)S(1)}, f32[128,128]{0,1:T(8,128)}, u32[]{:S(2)}, u32[]{:S(2)}) collective-permute-start(f32[128,128]{0,1:T(8,128)S(1)} %fusion.64), channel_id=1, source_target_pairs={{0,3},{1,2},{2,1},{3,0},{4,7},{5,6},{6,5},{7,4},{8,11},{9,10},{10,... | collective-permute-start | bytes 196616 | tf_op jit(solution)/shard_map/ppermute | solution.py:56
  57.4 38.9 %collective-permute-start.9 = (f32[128,128]{0,1:T(8,128)S(1)}, f32[128,128]{0,1:T(8,128)}, u32[]{:S(2)}, u32[]{:S(2)}) collective-permute-start(f32[128,128]{0,1:T(8,128)S(1)} %fusion.64), channel_id=1, source_target_pairs={{0,1},{1,0},{2,3},{3,2},{4,5},{5,4},{6,7},{7,6},{8,9},{9,8},{10,11... | collective-permute-start | bytes 196616 | tf_op jit(solution)/shard_map/ppermute | solution.py:56
  93.2 16.9 %copy-start.8 = (f32[128]{0:T(128)S(1)}, f32[128]{0:T(128)}, u32[]{:S(2)}) copy-start(f32[128]{0:T(128)} %get-tuple-element.71) | copy-start | bytes 1540
  94.5 8.3 %collective-permute-start.17 = (f32[128,256]{0,1:T(8,128)S(1)}, f32[128,256]{0,1:T(8,128)S(1)}, u32[]{:S(2)}, u32[]{:S(2)}) collective-permute-start(f32[128,256]{0,1:T(8,128)S(1)} %fusion.9), channel_id=1, source_target_pairs={{0,3},{1,2},{2,1},{3,0},{4,7},{5,6},{6,5},{7,4},{8,11},{9,10},{10,... | collective-permute-start | bytes 393224 | tf_op jit(solution)/shard_map/ppermute | solution.py:56
  95.1 41.3 %collective-permute-start.5 = (f32[2,2,2,184,256]{4,3,2,1,0:T(8,128)}, f32[2,2,2,184,256]{4,3,2,1,0:T(8,128)}, u32[]{:S(2)}, u32[]{:S(2)}) collective-permute-start(f32[2,2,2,184,256]{4,3,2,1,0:T(8,128)} %dynamic-slice_bitcast_fusion), channel_id=1, source_target_pairs={{0,1},{1,0},{2,3},{3,2},{4,5},{5,4},{6,7},{7,6},{8,9},{9,8},{10,11... | collective-permute-start | bytes 4521992 | tf_op jit(solution)/shard_map/ppermute | solution.py:106
  97.2 6.7 %collective-permute-start.12 = (f32[128,128]{0,1:T(8,128)S(1)}, f32[128,128]{0,1:T(8,128)S(1)}, u32[]{:S(2)}, u32[]{:S(2)}) collective-permute-start(f32[128,128]{0,1:T(8,128)S(1)} %add_add_fusion.2), channel_id=1, source_target_pairs={{0,4},{1,5},{2,6},{3,7},{4,0},{5,1},{6,2},{7,3},{8,12},{9,13},{10,... | collective-permute-start | bytes 196616 | tf_op jit(solution)/shard_map/ppermute | solution.py:56
  99.2 9.3 %collective-permute-start.13 = (f32[128,128]{0,1:T(8,128)S(1)}, f32[128,128]{0,1:T(8,128)S(1)}, u32[]{:S(2)}, u32[]{:S(2)}) collective-permute-start(f32[128,128]{0,1:T(8,128)S(1)} %add_add_fusion.2), channel_id=1, source_target_pairs={{0,8},{1,9},{2,10},{3,11},{4,12},{5,13},{6,14},{7,15},{8,0},{9,1},... | collective-permute-start | bytes 196616 | tf_op jit(solution)/shard_map/ppermute | solution.py:56
  102.8 7.2 %collective-permute-start.14 = (f32[128,128]{0,1:T(8,128)S(1)}, f32[128,128]{0,1:T(8,128)S(1)}, u32[]{:S(2)}, u32[]{:S(2)}) collective-permute-start(f32[128,128]{0,1:T(8,128)S(1)} %add_add_fusion.2), channel_id=1, source_target_pairs={{0,12},{1,13},{2,14},{3,15},{4,8},{5,9},{6,10},{7,11},{8,4},{9,5},... | collective-permute-start | bytes 196616 | tf_op jit(solution)/shard_map/ppermute | solution.py:56
  103.8 35.6 %collective-permute-start.18 = (f32[128,256]{0,1:T(8,128)S(1)}, f32[128,256]{0,1:T(8,128)S(1)}, u32[]{:S(2)}, u32[]{:S(2)}) collective-permute-start(f32[128,256]{0,1:T(8,128)S(1)} %add_add_fusion.1), channel_id=1, source_target_pairs={{0,4},{1,5},{2,6},{3,7},{4,0},{5,1},{6,2},{7,3},{8,12},{9,13},{10,... | collective-permute-start | bytes 393224 | tf_op jit(solution)/shard_map/ppermute | solution.py:56
  103.9 35.5 %collective-permute-start.19 = (f32[128,256]{0,1:T(8,128)S(1)}, f32[128,256]{0,1:T(8,128)S(1)}, u32[]{:S(2)}, u32[]{:S(2)}) collective-permute-start(f32[128,256]{0,1:T(8,128)S(1)} %add_add_fusion.1), channel_id=1, source_target_pairs={{0,8},{1,9},{2,10},{3,11},{4,12},{5,13},{6,14},{7,15},{8,0},{9,1},... | collective-permute-start | bytes 393224 | tf_op jit(solution)/shard_map/ppermute | solution.py:56
  108.6 30.8 %collective-permute-start.20 = (f32[128,256]{0,1:T(8,128)S(1)}, f32[128,256]{0,1:T(8,128)}, u32[]{:S(2)}, u32[]{:S(2)}) collective-permute-start(f32[128,256]{0,1:T(8,128)S(1)} %add_add_fusion.1), channel_id=1, source_target_pairs={{0,12},{1,13},{2,14},{3,15},{4,8},{5,9},{6,10},{7,11},{8,4},{9,5},... | collective-permute-start | bytes 393224 | tf_op jit(solution)/shard_map/ppermute | solution.py:56
  136.4 3.9 %copy-start.9 = (f32[128]{0:T(128)S(1)}, f32[128]{0:T(128)}, u32[]{:S(2)}) copy-start(f32[128]{0:T(128)} %get-tuple-element.52) | copy-start | bytes 1540
  136.4 3.9 %copy-start.10 = (f32[128]{0:T(128)S(1)}, f32[128]{0:T(128)}, u32[]{:S(2)}) copy-start(f32[128]{0:T(128)} %get-tuple-element.53) | copy-start | bytes 1540
  136.4 3.9 %copy-start.11 = (f32[128]{0:T(128)S(1)}, f32[128]{0:T(128)}, u32[]{:S(2)}) copy-start(f32[128]{0:T(128)} %get-tuple-element.54) | copy-start | bytes 1540
  136.5 4.3 %copy-start.12 = (f32[128]{0:T(128)S(1)}, f32[128]{0:T(128)}, u32[]{:S(2)}) copy-start(f32[128]{0:T(128)} %get-tuple-element.51) | copy-start | bytes 1540
  138.1 1.2 copy-start
  139.3 14.1 %collective-permute-start.6 = (f32[2,2,184,256]{3,2,1,0:T(8,128)S(1)}, f32[2,2,184,256]{3,2,1,0:T(8,128)S(1)}, u32[]{:S(2)}, u32[]{:S(2)}) collective-permute-start(f32[2,2,184,256]{3,2,1,0:T(8,128)S(1)} %dynamic-slice_bitcast_fusion.1), channel_id=1, source_target_pairs={{0,4},{1,5},{2,6},{3,7},{4,0},{5,1},{6,2},{7,3},{8,12},{9,13},{10,... | collective-permute-start | bytes 2261000 | tf_op jit(solution)/shard_map/ppermute | solution.py:106
  154.6 22.0 %copy-start.5 = (f32[1,184]{1,0:T(1,128)S(1)}, f32[1,184]{1,0:T(1,128)}, u32[]{:S(2)}) copy-start(f32[1,184]{1,0:T(1,128)} %get-tuple-element.66) | copy-start | bytes 2212
  154.6 22.0 %copy-start.6 = (f32[1,184]{1,0:T(1,128)S(1)}, f32[1,184]{1,0:T(1,128)}, u32[]{:S(2)}) copy-start(f32[1,184]{1,0:T(1,128)} %get-tuple-element.67) | copy-start | bytes 2212
  154.7 22.1 %copy-start.7 = (f32[128]{0:T(128)S(1)}, f32[128]{0:T(128)}, u32[]{:S(2)}) copy-start(f32[128]{0:T(128)} %slice.232) | copy-start | bytes 1540
  154.9 13.9 %collective-permute-start.7 = (f32[2,184,256]{1,2,0:T(8,128)S(1)}, f32[2,184,256]{1,2,0:T(8,128)S(1)}, u32[]{:S(2)}, u32[]{:S(2)}) collective-permute-start(f32[2,184,256]{1,2,0:T(8,128)S(1)} %bitcast.128), channel_id=1, source_target_pairs={{0,3},{1,2},{2,1},{3,0},{4,7},{5,6},{6,5},{7,4},{8,11},{9,10},{10,... | collective-permute-start | bytes 1130504 | tf_op jit(solution)/shard_map/ppermute | solution.py:106
  168.9 7.7 %collective-permute-start.8 = (f32[184,256]{0,1:T(8,128)S(1)}, f32[184,256]{0,1:T(8,128)S(1)}, u32[]{:S(2)}, u32[]{:S(2)}) collective-permute-start(f32[184,256]{0,1:T(8,128)S(1)} %dynamic-slice_bitcast_fusion.2), channel_id=1, source_target_pairs={{0,12},{1,13},{2,14},{3,15},{4,8},{5,9},{6,10},{7,11},{8,4},{9,5},... | collective-permute-start | bytes 565256 | tf_op jit(solution)/shard_map/ppermute | solution.py:106
  (2 other events, 2.0 us)
where the time goes:
time: 180 us; the launch traced here: 179 us
  other arithmetic  61.5 us (34%)
  waiting for transfers between devices  35.3 us (20%)
  starting transfers between devices  32.4 us (18%)
  matrix products  32.1 us (18%)
  local copies, waits for them, and re-layouts  16.9 us (9%)
    dot_general x8, matrix products, times_transposed(): lax.dot_general(left_mat, right_mat, (((1,), (1,)), ((), ())), precision=...  30.7 us
    ppermute x1, waiting for transfers between devices, row_broadcast(): relay = lax.ppermute(first_out, 'row', [(2, 4), (7, 5)])  27.8 us
    another operation x6, other arithmetic, lower_inverse(): factor = jnp.linalg.cholesky(square)  25.6 us
    another operation x4, other arithmetic, lower_inverse(): jax.scipy.linalg.solve_triangular(factor, jnp.eye(square.shape[0], dtype=...  21.6 us
    ppermute x12, starting transfers between devices, col_sum(): lax.ppermute(block, 'col', [(i, i ^ k * group) for i in range(count)])  19.1 us
    ppermute x4, starting transfers between devices, col_scatter(): shaped = keep + lax.ppermute(send, 'col', perm)  6.81 us
    slice x5, local copies, waits for them, and re-layouts, col_scatter(): shaped = jnp.stack([shaped[z] for z in order])  5.27 us
    ppermute x4, waiting for transfers between devices, col_scatter(): shaped = keep + lax.ppermute(send, 'col', perm)  4.88 us
  transfers between devices with their start and end apart: 21, of which 5 were waited for; matrix products, arithmetic and copies ran while one was open for 53% of the time, Pallas kernels for 0%

commit v1 on v0

--- a/solution.py
+++ b/solution.py
@@ -100,11 +100,17 @@
         (1, my_y >> 1, pairs(lambda z, y: z * ring + (ring - 1 - y))),
         (0, my_z >> 1, pairs(lambda z, y: (ring - 1 - z) * ring + y)),
     )
-    for axis, mine, perm in steps:
+    for axis, mine, perm in steps[:-1]:
         keep = lax.dynamic_index_in_dim(shaped, mine, axis, keepdims=False)
         send = lax.dynamic_index_in_dim(shaped, 1 - mine, axis, keepdims=False)
         shaped = keep + lax.ppermute(send, "col", perm)
-    return shaped
+    axis, mine, perm = steps[-1]
+    keep = lax.dynamic_index_in_dim(shaped, mine, axis, keepdims=False)
+    send = lax.dynamic_index_in_dim(shaped, 1 - mine, axis, keepdims=False)
+    cut = send.shape[-1] // 2
+    first = keep[..., :cut] + lax.ppermute(send[..., :cut], "col", perm)
+    second = keep[..., cut:] + lax.ppermute(send[..., cut:], "col", perm)
+    return first, second
 
 
 def body(left_factor, pick_site, noise):
@@ -148,7 +154,7 @@
     terms = times_transposed(local_rows, heads, lax.Precision.HIGH).reshape(
         col_count, row_share, 2 * block_width
     )
-    sums = col_scatter(terms)
+    first_sums, second_sums = col_scatter(terms)
 
     first_coords = info[:3, :block_width]
     second_coords = info[:3, block_width:]
@@ -166,11 +172,11 @@
     second_diag = second_diag + jnp.diag(info[3, block_width:])
     second_inverse = lower_inverse(second_diag)
 
-    first_cov = matern(my_coords, first_coords) - sums[:, :block_width]
+    first_cov = matern(my_coords, first_coords) - first_sums
     first_cov = first_cov.at[:block_width].add(jnp.where(first_owner, own_diag, 0.0))
     first_panel = times_transposed(first_cov, first_inverse)
     second_cov = (
-        (matern(my_coords, second_coords) - sums[:, block_width:])
+        (matern(my_coords, second_coords) - second_sums)
         - times_transposed(first_panel, cross_rows)
     )
     second_cov = second_cov.at[:block_width].add(jnp.where(second_owner, own_diag, 0.0))

time: 180 us -> 181 us (level)
    ppermute x0 -> x2, waiting for transfers between devices: none -> 5.22 us  [the longest x1 2.65 us: col_scatter(): second = keep[..., cut:] + lax.ppermute(send[..., cut:], 'col', perm)]
    ppermute x4 -> x3, waiting for transfers between devices: 4.88 us -> 0.57 us  [col_scatter(): shaped = keep + lax.ppermute(send, 'col', perm)]
    ppermute x0 -> x2, starting transfers between devices: none -> 3.4 us  [the longest x1 3.02 us: col_scatter(): first = keep[..., :cut] + lax.ppermute(send[..., :cut], 'col', perm)]
    ppermute x4 -> x3, starting transfers between devices: 6.81 us -> 3.8 us  [col_scatter(): shaped = keep + lax.ppermute(send, 'col', perm)]
  transfers between devices with their start and end apart: 21 -> 22, of which waited for: 5 -> 6; matrix products, arithmetic and copies ran while one was open for 53% -> 53% of each run, Pallas kernels for 0% -> 0%
where the time goes in v1:
time: 181 us
  other arithmetic  61.4 us (34%)
  waiting for transfers between devices  36.3 us (20%)
  starting transfers between devices  32.7 us (18%)
  matrix products  32.1 us (18%)
  local copies, waits for them, and re-layouts  17.4 us (10%)
    dot_general x8, matrix products, times_transposed(): lax.dot_general(left_mat, right_mat, (((1,), (1,)), ((), ())), precision=...  30.7 us
    ppermute x1, waiting for transfers between devices, row_broadcast(): relay = lax.ppermute(first_out, 'row', [(2, 4), (7, 5)])  27.8 us
    another operation x6, other arithmetic, lower_inverse(): factor = jnp.linalg.cholesky(square)  25.6 us
    another operation x4, other arithmetic, lower_inverse(): jax.scipy.linalg.solve_triangular(factor, jnp.eye(square.shape[0], dtype=...  21.6 us
    ppermute x12, starting transfers between devices, col_sum(): lax.ppermute(block, 'col', [(i, i ^ k * group) for i in range(count)])  19.1 us
    slice x5, local copies, waits for them, and re-layouts, col_scatter(): shaped = jnp.stack([shaped[z] for z in order])  5.25 us
    slice x1, local copies, waits for them, and re-layouts, body(): head_rows = local_rows[:block_width]  3.97 us
    ppermute x3, starting transfers between devices, col_scatter(): shaped = keep + lax.ppermute(send, 'col', perm)  3.8 us
  transfers between devices with their start and end apart: 22, of which 6 were waited for; matrix products, arithmetic and copies ran while one was open for 53% of the time, Pallas kernels for 0%

profile of v1, /device:TPU:4, one launch (start us, length us, event | category | flops | bytes accessed | tf_op | source)
XLA Modules:
  0.0 180.6 jit_solution(14764769790968817379)
XLA Ops:
  1.3 4.0 %slice_reduce_fusion = f32[128,16,128]{2,1,0:T(8,128)S(1)} fusion(f32[23,1,128,16,1,128]{5,4,3,2,1,0:T(1,128)} %param.12), kind=kLoop, calls=%fused_computation.28 | loop fusion | bytes 2097152 | tf_op jit(solution)/shard_map/slice | solution.py:132
  6.8 1.1 broadcast_select_fusion.1
  8.8 1.3 collective-permute-start.1
  10.1 1.7 collective-permute-start.3
  12.8 27.8 %collective-permute-done.1 = f32[136,2048]{1,0:T(8,128)} collective-permute-done((f32[136,2048]{1,0:T(8,128)S(1)}, f32[136,2048]{1,0:T(8,128)}, u32[]{:S(2)}, u32[]{:S(2)}) %collective-permute-start.1) | collective-permute-done | bytes 1114144 | tf_op jit(solution)/shard_map/ppermute | solution.py:69
  40.6 1.6 select_select_fusion
  42.2 1.9 %collective-permute-start.4 = (f32[136,2048]{1,0:T(8,128)S(1)}, f32[136,2048]{1,0:T(8,128)S(1)}, u32[]{:S(2)}, u32[]{:S(2)}) collective-permute-start(f32[136,2048]{1,0:T(8,128)S(1)} %select_select_fusion), channel_id=1, source_target_pairs={{32,48},{48,32},{64,80},{80,64},{96,112},{112,96},{33,49},{49,33},... | collective-permute-start | bytes 3342344 | tf_op jit(solution)/shard_map/ppermute | solution.py:78
  45.6 1.2 collective-permute-done.4
  47.2 1.8 fusion.9
  49.0 1.7 collective-permute-start.16
  50.7 2.9 %collective-permute-start.17 = (f32[128,256]{0,1:T(8,128)S(1)}, f32[128,256]{0,1:T(8,128)}, u32[]{:S(2)}, u32[]{:S(2)}) collective-permute-start(f32[128,256]{0,1:T(8,128)S(1)} %fusion.9), channel_id=1, source_target_pairs={{0,2},{1,3},{2,0},{3,1},{4,6},{5,7},{6,4},{7,5},{8,10},{9,11},{10,... | collective-permute-start | bytes 393224 | tf_op jit(solution)/shard_map/ppermute | solution.py:56
  55.3 2.2 %collective-permute-start.11 = (f32[128,128]{0,1:T(8,128)S(1)}, f32[128,128]{0,1:T(8,128)}, u32[]{:S(2)}, u32[]{:S(2)}) collective-permute-start(f32[128,128]{0,1:T(8,128)S(1)} %fusion.66), channel_id=1, source_target_pairs={{0,3},{1,2},{2,1},{3,0},{4,7},{5,6},{6,5},{7,4},{8,11},{9,10},{10,... | collective-permute-start | bytes 196616 | tf_op jit(solution)/shard_map/ppermute | solution.py:56
  59.3 26.0 %fusion.3 = f32[2944,256]{0,1:T(8,128)S(1)} fusion(f32[368,8,16,128]{3,2,1,0:T(8,128)} %bitcast.117, f32[128,2048]{1,0:T(8,128)S(1)} %slice.254, f32[128,2048]{1,0:T(8,128)S(1)} %slice.253), kind=kOutput, calls=%fused_computation.5 | convolution fusion | flops 9261547520 | bytes 29229056 | tf_op jit(solution)/shard_map/dot_general | solution.py:34
  86.0 1.1 copy.17
  88.3 1.2 copy.19
  90.6 3.1 %fusion.6 = f32[4,4,184,256]{3,2,1,0:T(8,128)S(1)} fusion(f32[1,4,184,256]{3,2,1,0:T(8,128)} %bitcast.127, f32[1,4,184,256]{3,2,1,0:T(8,128)} %bitcast.126, f32[1,4,184,256]{3,2,1,0:T(8,128)} %bitcast.125, f32[1,4,184,256]{3,2,1,0:T(8,128)} %bitcast.124), kind=kLoop, calls=%fused_computation.7 | loop fusion | flops 21102592 | bytes 6029312 | tf_op jit(solution)/shard_map/stack | solution.py:90
  93.7 1.3 dynamic-slice_bitcast_fusion
  95.6 1.2 collective-permute-start.5
  97.7 2.0 %collective-permute-start.12 = (f32[128,128]{0,1:T(8,128)S(1)}, f32[128,128]{0,1:T(8,128)S(1)}, u32[]{:S(2)}, u32[]{:S(2)}) collective-permute-start(f32[128,128]{0,1:T(8,128)S(1)} %add_add_fusion.2), channel_id=1, source_target_pairs={{0,4},{1,5},{2,6},{3,7},{4,0},{5,1},{6,2},{7,3},{8,12},{9,13},{10,... | collective-permute-start | bytes 196616 | tf_op jit(solution)/shard_map/ppermute | solution.py:56
  99.7 3.6 %collective-permute-start.13 = (f32[128,128]{0,1:T(8,128)S(1)}, f32[128,128]{0,1:T(8,128)S(1)}, u32[]{:S(2)}, u32[]{:S(2)}) collective-permute-start(f32[128,128]{0,1:T(8,128)S(1)} %add_add_fusion.2), channel_id=1, source_target_pairs={{0,8},{1,9},{2,10},{3,11},{4,12},{5,13},{6,14},{7,15},{8,0},{9,1},... | collective-permute-start | bytes 196616 | tf_op jit(solution)/shard_map/ppermute | solution.py:56
  104.4 4.7 %collective-permute-start.20 = (f32[128,256]{0,1:T(8,128)S(1)}, f32[128,256]{0,1:T(8,128)S(1)}, u32[]{:S(2)}, u32[]{:S(2)}) collective-permute-start(f32[128,256]{0,1:T(8,128)S(1)} %add_add_fusion.1), channel_id=1, source_target_pairs={{0,8},{1,9},{2,10},{3,11},{4,12},{5,13},{6,14},{7,15},{8,0},{9,1},... | collective-permute-start | bytes 393224 | tf_op jit(solution)/shard_map/ppermute | solution.py:56
  109.0 1.5 collective-permute-done.14
  111.4 12.5 %cholesky.44 = f32[128,128]{1,0:T(8,128)S(1)} custom-call(f32[128,128]{1,0:T(8,128)} %fusion.29), custom_call_target="Cholesky" | custom-call | tf_op jit(solution)/shard_map/jit(cholesky)/cholesky | solution.py:44
  125.3 10.4 %custom-call.6 = f32[1,128,128]{1,2,0:T(8,128)} custom-call(f32[1,128,128]{2,1,0:T(8,128)S(1)} %fusion.17), custom_call_target="InvertDiagBlocksLowerTriangular" | custom-call | tf_op jit(solution)/shard_map/jit(_solve_triangular)/triangular_solve | solution.py:45
  136.9 1.6 bitcast_add_fusion
  141.6 11.7 %cholesky.55 = f32[128,128]{1,0:T(8,128)S(1)} custom-call(f32[128,128]{1,0:T(8,128)S(1)} %fusion.27), custom_call_target="Cholesky" | custom-call | tf_op jit(solution)/shard_map/jit(cholesky)/cholesky | solution.py:44
  153.9 1.2 bitcast_add_fusion.1
  155.4 2.5 %collective-permute-start.7 = (f32[2,184,256]{1,2,0:T(8,128)S(1)}, f32[2,184,256]{1,2,0:T(8,128)S(1)}, u32[]{:S(2)}, u32[]{:S(2)}) collective-permute-start(f32[2,184,256]{1,2,0:T(8,128)S(1)} %bitcast.128), channel_id=1, source_target_pairs={{0,3},{1,2},{2,1},{3,0},{4,7},{5,6},{6,5},{7,4},{8,11},{9,10},{10,... | collective-permute-start | bytes 1130504 | tf_op jit(solution)/shard_map/ppermute | solution.py:106
  159.3 9.8 %custom-call.7 = f32[1,128,128]{1,2,0:T(8,128)S(1)} custom-call(f32[1,128,128]{2,1,0:T(8,128)S(1)} %fusion.18), custom_call_target="InvertDiagBlocksLowerTriangular" | custom-call | tf_op jit(solution)/shard_map/jit(_solve_triangular)/triangular_solve | solution.py:45
  169.5 3.0 %collective-permute-start.8 = (f32[184,128]{0,1:T(8,128)S(1)}, f32[184,128]{0,1:T(8,128)S(1)}, u32[]{:S(2)}, u32[]{:S(2)}) collective-permute-start(f32[184,128]{0,1:T(8,128)S(1)} %get-tuple-element.64), channel_id=1, source_target_pairs={{0,12},{1,13},{2,14},{3,15},{4,8},{5,9},{6,10},{7,11},{8,4},{9,5},... | collective-permute-start | bytes 282632 | tf_op jit(solution)/shard_map/ppermute | solution.py:111
  173.1 2.6 %collective-permute-done.8 = f32[184,128]{0,1:T(8,128)S(1)} collective-permute-done((f32[184,128]{0,1:T(8,128)S(1)}, f32[184,128]{0,1:T(8,128)S(1)}, u32[]{:S(2)}, u32[]{:S(2)}) %collective-permute-start.8) | collective-permute-done | bytes 94240 | tf_op jit(solution)/shard_map/ppermute | solution.py:111
  176.4 2.6 %collective-permute-done.15 = f32[184,128]{0,1:T(8,128)S(1)} collective-permute-done((f32[184,128]{0,1:T(8,128)S(1)}, f32[184,128]{0,1:T(8,128)S(1)}, u32[]{:S(2)}, u32[]{:S(2)}) %collective-permute-start.15) | collective-permute-done | bytes 94240 | tf_op jit(solution)/shard_map/ppermute | solution.py:112
  (108 shorter events, 27.2 us)
Async XLA Ops:
  5.8 0.8 collective-permute-start
  8.0 36.2 %copy-start.3 = (s32[23,1,128]{2,1,0:T(1,128)S(1)}, s32[23,1,128]{2,1,0:T(1,128)}, u32[]{:S(2)}) copy-start(s32[23,1,128]{2,1,0:T(1,128)} %param.13) | copy-start | bytes 35332
  8.0 36.3 %copy-start.4 = (f32[23,1,128]{2,1,0:T(1,128)S(1)}, f32[23,1,128]{2,1,0:T(1,128)}, u32[]{:S(2)}) copy-start(f32[23,1,128]{2,1,0:T(1,128)} %param.14) | copy-start | bytes 35332
  8.0 3.8 %collective-permute-start.2 = (f32[136,2048]{1,0:T(8,128)}, f32[136,2048]{1,0:T(8,128)S(1)}, u32[]{:S(2)}, u32[]{:S(2)}) collective-permute-start(f32[136,2048]{1,0:T(8,128)} %broadcast_select_fusion.1), channel_id=1, source_target_pairs={{16,48},{0,96},{17,49},{1,97},{18,50},{2,98},{19,51},{3,99},{20,52... | collective-permute-start | bytes 3342344 | tf_op jit(solution)/shard_map/ppermute | solution.py:70
  8.8 31.8 %collective-permute-start.1 = (f32[136,2048]{1,0:T(8,128)S(1)}, f32[136,2048]{1,0:T(8,128)}, u32[]{:S(2)}, u32[]{:S(2)}) collective-permute-start(f32[136,2048]{1,0:T(8,128)S(1)} %collective-permute-done), channel_id=1, source_target_pairs={{32,64},{112,80},{33,65},{113,81},{34,66},{114,82},{35,67},{115,83... | collective-permute-start | bytes 3342344 | tf_op jit(solution)/shard_map/ppermute | solution.py:69
  10.1 35.5 %collective-permute-start.3 = (f32[136,2048]{1,0:T(8,128)}, f32[136,2048]{1,0:T(8,128)}, u32[]{:S(2)}, u32[]{:S(2)}) collective-permute-start(f32[136,2048]{1,0:T(8,128)} %copy-done.2), channel_id=1, source_target_pairs={{0,16},{16,0},{1,17},{17,1},{2,18},{18,2},{3,19},{19,3},{4,20},{20... | collective-permute-start | bytes 3342344 | tf_op jit(solution)/shard_map/ppermute | solution.py:67
  42.2 4.6 %collective-permute-start.4 = (f32[136,2048]{1,0:T(8,128)S(1)}, f32[136,2048]{1,0:T(8,128)S(1)}, u32[]{:S(2)}, u32[]{:S(2)}) collective-permute-start(f32[136,2048]{1,0:T(8,128)S(1)} %select_select_fusion), channel_id=1, source_target_pairs={{32,48},{48,32},{64,80},{80,64},{96,112},{112,96},{33,49},{49,33},... | collective-permute-start | bytes 3342344 | tf_op jit(solution)/shard_map/ppermute | solution.py:78
  49.0 50.7 %collective-permute-start.16 = (f32[128,256]{0,1:T(8,128)S(1)}, f32[128,256]{0,1:T(8,128)S(1)}, u32[]{:S(2)}, u32[]{:S(2)}) collective-permute-start(f32[128,256]{0,1:T(8,128)S(1)} %fusion.9), channel_id=1, source_target_pairs={{0,1},{1,0},{2,3},{3,2},{4,5},{5,4},{6,7},{7,6},{8,9},{9,8},{10,11... | collective-permute-start | bytes 393224 | tf_op jit(solution)/shard_map/ppermute | solution.py:56
  50.7 52.6 %collective-permute-start.17 = (f32[128,256]{0,1:T(8,128)S(1)}, f32[128,256]{0,1:T(8,128)}, u32[]{:S(2)}, u32[]{:S(2)}) collective-permute-start(f32[128,256]{0,1:T(8,128)S(1)} %fusion.9), channel_id=1, source_target_pairs={{0,2},{1,3},{2,0},{3,1},{4,6},{5,7},{6,4},{7,5},{8,10},{9,11},{10,... | collective-permute-start | bytes 393224 | tf_op jit(solution)/shard_map/ppermute | solution.py:56
  54.6 40.4 %collective-permute-start.10 = (f32[128,128]{0,1:T(8,128)S(1)}, f32[128,128]{0,1:T(8,128)S(1)}, u32[]{:S(2)}, u32[]{:S(2)}) collective-permute-start(f32[128,128]{0,1:T(8,128)S(1)} %fusion.66), channel_id=1, source_target_pairs={{0,2},{1,3},{2,0},{3,1},{4,6},{5,7},{6,4},{7,5},{8,10},{9,11},{10,... | collective-permute-start | bytes 196616 | tf_op jit(solution)/shard_map/ppermute | solution.py:56
  55.3 40.3 %collective-permute-start.11 = (f32[128,128]{0,1:T(8,128)S(1)}, f32[128,128]{0,1:T(8,128)}, u32[]{:S(2)}, u32[]{:S(2)}) collective-permute-start(f32[128,128]{0,1:T(8,128)S(1)} %fusion.66), channel_id=1, source_target_pairs={{0,3},{1,2},{2,1},{3,0},{4,7},{5,6},{6,5},{7,4},{8,11},{9,10},{10,... | collective-permute-start | bytes 196616 | tf_op jit(solution)/shard_map/ppermute | solution.py:56
  57.5 39.3 %collective-permute-start.9 = (f32[128,128]{0,1:T(8,128)S(1)}, f32[128,128]{0,1:T(8,128)}, u32[]{:S(2)}, u32[]{:S(2)}) collective-permute-start(f32[128,128]{0,1:T(8,128)S(1)} %fusion.66), channel_id=1, source_target_pairs={{0,1},{1,0},{2,3},{3,2},{4,5},{5,4},{6,7},{7,6},{8,9},{9,8},{10,11... | collective-permute-start | bytes 196616 | tf_op jit(solution)/shard_map/ppermute | solution.py:56
  93.7 16.8 %copy-start.8 = (f32[128]{0:T(128)S(1)}, f32[128]{0:T(128)}, u32[]{:S(2)}) copy-start(f32[128]{0:T(128)} %get-tuple-element.55) | copy-start | bytes 1540
  95.0 8.3 %collective-permute-start.18 = (f32[128,256]{0,1:T(8,128)S(1)}, f32[128,256]{0,1:T(8,128)S(1)}, u32[]{:S(2)}, u32[]{:S(2)}) collective-permute-start(f32[128,256]{0,1:T(8,128)S(1)} %fusion.9), channel_id=1, source_target_pairs={{0,3},{1,2},{2,1},{3,0},{4,7},{5,6},{6,5},{7,4},{8,11},{9,10},{10,... | collective-permute-start | bytes 393224 | tf_op jit(solution)/shard_map/ppermute | solution.py:56
  95.6 41.3 %collective-permute-start.5 = (f32[2,2,2,184,256]{4,3,2,1,0:T(8,128)}, f32[2,2,2,184,256]{4,3,2,1,0:T(8,128)}, u32[]{:S(2)}, u32[]{:S(2)}) collective-permute-start(f32[2,2,2,184,256]{4,3,2,1,0:T(8,128)} %dynamic-slice_bitcast_fusion), channel_id=1, source_target_pairs={{0,1},{1,0},{2,3},{3,2},{4,5},{5,4},{6,7},{7,6},{8,9},{9,8},{10,11... | collective-permute-start | bytes 4521992 | tf_op jit(solution)/shard_map/ppermute | solution.py:106
  97.7 6.7 %collective-permute-start.12 = (f32[128,128]{0,1:T(8,128)S(1)}, f32[128,128]{0,1:T(8,128)S(1)}, u32[]{:S(2)}, u32[]{:S(2)}) collective-permute-start(f32[128,128]{0,1:T(8,128)S(1)} %add_add_fusion.2), channel_id=1, source_target_pairs={{0,4},{1,5},{2,6},{3,7},{4,0},{5,1},{6,2},{7,3},{8,12},{9,13},{10,... | collective-permute-start | bytes 196616 | tf_op jit(solution)/shard_map/ppermute | solution.py:56
  99.7 9.3 %collective-permute-start.13 = (f32[128,128]{0,1:T(8,128)S(1)}, f32[128,128]{0,1:T(8,128)S(1)}, u32[]{:S(2)}, u32[]{:S(2)}) collective-permute-start(f32[128,128]{0,1:T(8,128)S(1)} %add_add_fusion.2), channel_id=1, source_target_pairs={{0,8},{1,9},{2,10},{3,11},{4,12},{5,13},{6,14},{7,15},{8,0},{9,1},... | collective-permute-start | bytes 196616 | tf_op jit(solution)/shard_map/ppermute | solution.py:56
  103.3 7.2 %collective-permute-start.14 = (f32[128,128]{0,1:T(8,128)S(1)}, f32[128,128]{0,1:T(8,128)S(1)}, u32[]{:S(2)}, u32[]{:S(2)}) collective-permute-start(f32[128,128]{0,1:T(8,128)S(1)} %add_add_fusion.2), channel_id=1, source_target_pairs={{0,12},{1,13},{2,14},{3,15},{4,8},{5,9},{6,10},{7,11},{8,4},{9,5},... | collective-permute-start | bytes 196616 | tf_op jit(solution)/shard_map/ppermute | solution.py:56
  104.3 35.6 %collective-permute-start.19 = (f32[128,256]{0,1:T(8,128)S(1)}, f32[128,256]{0,1:T(8,128)S(1)}, u32[]{:S(2)}, u32[]{:S(2)}) collective-permute-start(f32[128,256]{0,1:T(8,128)S(1)} %add_add_fusion.1), channel_id=1, source_target_pairs={{0,4},{1,5},{2,6},{3,7},{4,0},{5,1},{6,2},{7,3},{8,12},{9,13},{10,... | collective-permute-start | bytes 393224 | tf_op jit(solution)/shard_map/ppermute | solution.py:56
  104.4 35.5 %collective-permute-start.20 = (f32[128,256]{0,1:T(8,128)S(1)}, f32[128,256]{0,1:T(8,128)S(1)}, u32[]{:S(2)}, u32[]{:S(2)}) collective-permute-start(f32[128,256]{0,1:T(8,128)S(1)} %add_add_fusion.1), channel_id=1, source_target_pairs={{0,8},{1,9},{2,10},{3,11},{4,12},{5,13},{6,14},{7,15},{8,0},{9,1},... | collective-permute-start | bytes 393224 | tf_op jit(solution)/shard_map/ppermute | solution.py:56
  109.0 30.8 %collective-permute-start.21 = (f32[128,256]{0,1:T(8,128)S(1)}, f32[128,256]{0,1:T(8,128)}, u32[]{:S(2)}, u32[]{:S(2)}) collective-permute-start(f32[128,256]{0,1:T(8,128)S(1)} %add_add_fusion.1), channel_id=1, source_target_pairs={{0,12},{1,13},{2,14},{3,15},{4,8},{5,9},{6,10},{7,11},{8,4},{9,5},... | collective-permute-start | bytes 393224 | tf_op jit(solution)/shard_map/ppermute | solution.py:56
  136.9 3.9 %copy-start.9 = (f32[128]{0:T(128)S(1)}, f32[128]{0:T(128)}, u32[]{:S(2)}) copy-start(f32[128]{0:T(128)} %get-tuple-element.52) | copy-start | bytes 1540
  136.9 3.9 %copy-start.10 = (f32[128]{0:T(128)S(1)}, f32[128]{0:T(128)}, u32[]{:S(2)}) copy-start(f32[128]{0:T(128)} %get-tuple-element.53) | copy-start | bytes 1540
  136.9 3.9 %copy-start.11 = (f32[128]{0:T(128)S(1)}, f32[128]{0:T(128)}, u32[]{:S(2)}) copy-start(f32[128]{0:T(128)} %get-tuple-element.54) | copy-start | bytes 1540
  136.9 4.3 %copy-start.12 = (f32[128]{0:T(128)S(1)}, f32[128]{0:T(128)}, u32[]{:S(2)}) copy-start(f32[128]{0:T(128)} %get-tuple-element.51) | copy-start | bytes 1540
  139.7 14.2 %collective-permute-start.6 = (f32[2,2,184,256]{3,2,1,0:T(8,128)S(1)}, f32[2,2,184,256]{3,2,1,0:T(8,128)S(1)}, u32[]{:S(2)}, u32[]{:S(2)}) collective-permute-start(f32[2,2,184,256]{3,2,1,0:T(8,128)S(1)} %dynamic-slice_bitcast_fusion.1), channel_id=1, source_target_pairs={{0,4},{1,5},{2,6},{3,7},{4,0},{5,1},{6,2},{7,3},{8,12},{9,13},{10,... | collective-permute-start | bytes 2261000 | tf_op jit(solution)/shard_map/ppermute | solution.py:106
  155.2 20.5 %copy-start.5 = (f32[1,184]{1,0:T(1,128)S(1)}, f32[1,184]{1,0:T(1,128)}, u32[]{:S(2)}) copy-start(f32[1,184]{1,0:T(1,128)} %get-tuple-element.70) | copy-start | bytes 2212
  155.2 20.5 %copy-start.6 = (f32[1,184]{1,0:T(1,128)S(1)}, f32[1,184]{1,0:T(1,128)}, u32[]{:S(2)}) copy-start(f32[1,184]{1,0:T(1,128)} %get-tuple-element.71) | copy-start | bytes 2212
  155.2 20.7 %copy-start.7 = (f32[128]{0:T(128)S(1)}, f32[128]{0:T(128)}, u32[]{:S(2)}) copy-start(f32[128]{0:T(128)} %slice.239) | copy-start | bytes 1540
  155.4 13.9 %collective-permute-start.7 = (f32[2,184,256]{1,2,0:T(8,128)S(1)}, f32[2,184,256]{1,2,0:T(8,128)S(1)}, u32[]{:S(2)}, u32[]{:S(2)}) collective-permute-start(f32[2,184,256]{1,2,0:T(8,128)S(1)} %bitcast.128), channel_id=1, source_target_pairs={{0,3},{1,2},{2,1},{3,0},{4,7},{5,6},{6,5},{7,4},{8,11},{9,10},{10,... | collective-permute-start | bytes 1130504 | tf_op jit(solution)/shard_map/ppermute | solution.py:106
  169.5 6.3 %collective-permute-start.8 = (f32[184,128]{0,1:T(8,128)S(1)}, f32[184,128]{0,1:T(8,128)S(1)}, u32[]{:S(2)}, u32[]{:S(2)}) collective-permute-start(f32[184,128]{0,1:T(8,128)S(1)} %get-tuple-element.64), channel_id=1, source_target_pairs={{0,12},{1,13},{2,14},{3,15},{4,8},{5,9},{6,10},{7,11},{8,4},{9,5},... | collective-permute-start | bytes 282632 | tf_op jit(solution)/shard_map/ppermute | solution.py:111
  172.8 6.3 %collective-permute-start.15 = (f32[184,128]{0,1:T(8,128)S(1)}, f32[184,128]{0,1:T(8,128)S(1)}, u32[]{:S(2)}, u32[]{:S(2)}) collective-permute-start(f32[184,128]{0,1:T(8,128)S(1)} %get-tuple-element.63), channel_id=1, source_target_pairs={{0,12},{1,13},{2,14},{3,15},{4,8},{5,9},{6,10},{7,11},{8,4},{9,5},... | collective-permute-start | bytes 282632 | tf_op jit(solution)/shard_map/ppermute | solution.py:112
  (3 other events, 3.2 us)

commit v2 on v0

--- a/solution.py
+++ b/solution.py
@@ -129,16 +129,19 @@
     )
     is_first = row_index == 0
     is_second = row_index == 1
-    info_rows = jnp.zeros((8, head_rows.shape[1]), jnp.float32).at[:4, :block_width].set(head_info)
-    hand, other = row_broadcast(jnp.concatenate([head_rows, info_rows], axis=0))
+    head_flat = left_factor[0, 0].reshape(block_width * col_blocks, block_width)
+    info_rows = jnp.zeros((8, block_width), jnp.float32).at[:4].set(head_info)
+    hand, other = row_broadcast(jnp.concatenate([head_flat, info_rows], axis=0))
     is_even = row_index % 2 == 0
     first_pack = jnp.where(is_even, hand, other)
     second_pack = jnp.where(is_even, other, hand)
-    heads = jnp.concatenate([first_pack[:block_width], second_pack[:block_width]], axis=0)
+    flat_rows = block_width * col_blocks
+    heads = jnp.concatenate(
+        [first_pack[:flat_rows].reshape(block_width, -1), second_pack[:flat_rows].reshape(block_width, -1)],
+        axis=0,
+    )
     info = jnp.concatenate(
-        [first_pack[block_width : block_width + 4, :block_width],
-         second_pack[block_width : block_width + 4, :block_width]],
-        axis=1,
+        [first_pack[flat_rows : flat_rows + 4], second_pack[flat_rows : flat_rows + 4]], axis=1
     )
 
     gram_11 = col_sum(times_transposed(heads[:block_width], heads[:block_width]))

time: 180 us -> 174 us (0.967)
  other arithmetic: 61.5 us -> 59.6 us
  transfers between devices with their start and end apart: 21 -> 21, of which waited for: 5 -> 5; matrix products, arithmetic and copies ran while one was open for 53% -> 54% of each run, Pallas kernels for 0% -> 0%
where the time goes in v2:
time: 174 us
  other arithmetic  59.6 us (34%)
  waiting for transfers between devices  34.7 us (20%)
  starting transfers between devices  31.4 us (18%)
  matrix products  30.7 us (18%)
  local copies, waits for them, and re-layouts  16.9 us (10%)
    dot_general x8, matrix products, times_transposed(): lax.dot_general(left_mat, right_mat, (((1,), (1,)), ((), ())), precision=...  30.1 us
    ppermute x1, waiting for transfers between devices, row_broadcast(): relay = lax.ppermute(first_out, 'row', [(2, 4), (7, 5)])  27 us
    another operation x6, other arithmetic, lower_inverse(): factor = jnp.linalg.cholesky(square)  24.9 us
    another operation x4, other arithmetic, lower_inverse(): jax.scipy.linalg.solve_triangular(factor, jnp.eye(square.shape[0], dtype=...  21 us
    ppermute x12, starting transfers between devices, col_sum(): lax.ppermute(block, 'col', [(i, i ^ k * group) for i in range(count)])  18.1 us
    ppermute x4, starting transfers between devices, col_scatter(): shaped = keep + lax.ppermute(send, 'col', perm)  6.99 us
    ppermute x4, waiting for transfers between devices, col_scatter(): shaped = keep + lax.ppermute(send, 'col', perm)  6.05 us
    slice x5, local copies, waits for them, and re-layouts, col_scatter(): shaped = jnp.stack([shaped[z] for z in order])  5.23 us
  transfers between devices with their start and end apart: 21, of which 5 were waited for; matrix products, arithmetic and copies ran while one was open for 54% of the time, Pallas kernels for 0%

profile of v2, /device:TPU:4, one launch (start us, length us, event | category | flops | bytes accessed | tf_op | source)
XLA Modules:
  0.0 173.9 jit_solution(10920128909738787042)
XLA Ops:
  1.3 1.3 slice.200
  2.7 1.1 pad_maximum_fusion
  6.3 1.3 collective-permute-start.1
  7.6 1.6 collective-permute-start.3
  10.2 27.0 %collective-permute-done.1 = f32[2056,128]{1,0:T(8,128)} collective-permute-done((f32[2056,128]{1,0:T(8,128)S(1)}, f32[2056,128]{1,0:T(8,128)}, u32[]{:S(2)}, u32[]{:S(2)}) %collective-permute-start.1) | collective-permute-done | bytes 1052704 | tf_op jit(solution)/shard_map/ppermute | solution.py:69
  37.2 1.6 select_select_fusion
  38.8 1.9 %collective-permute-start.4 = (f32[2056,128]{1,0:T(8,128)S(1)}, f32[2056,128]{1,0:T(8,128)S(1)}, u32[]{:S(2)}, u32[]{:S(2)}) collective-permute-start(f32[2056,128]{1,0:T(8,128)S(1)} %select_select_fusion), channel_id=1, source_target_pairs={{32,48},{48,32},{64,80},{80,64},{96,112},{112,96},{33,49},{49,33},... | collective-permute-start | bytes 3158024 | tf_op jit(solution)/shard_map/ppermute | solution.py:78
  47.1 3.3 %collective-permute-start.10 = (f32[128,128]{0,1:T(8,128)S(1)}, f32[128,128]{0,1:T(8,128)S(1)}, u32[]{:S(2)}, u32[]{:S(2)}) collective-permute-start(f32[128,128]{0,1:T(8,128)S(1)} %fusion.62), channel_id=1, source_target_pairs={{0,2},{1,3},{2,0},{3,1},{4,6},{5,7},{6,4},{7,5},{8,10},{9,11},{10,... | collective-permute-start | bytes 196616 | tf_op jit(solution)/shard_map/ppermute | solution.py:56
  51.5 1.4 reshape.302
  53.0 1.8 %fusion.64 = f32[128,256]{0,1:T(8,128)S(1)} fusion(f32[128,2048]{1,0:T(8,128)S(1)} %reshape.302, f32[256,2048]{1,0:T(8,128)S(1)} %constant_dynamic-update-slice_fusion), kind=kOutput, calls=%fused_computation.158 | convolution fusion | flops 805306368 | bytes 3276800 | tf_op jit(solution)/shard_map/dot_general | solution.py:34
  54.8 3.1 %collective-permute-start.16 = (f32[128,256]{0,1:T(8,128)S(1)}, f32[128,256]{0,1:T(8,128)S(1)}, u32[]{:S(2)}, u32[]{:S(2)}) collective-permute-start(f32[128,256]{0,1:T(8,128)S(1)} %fusion.64), channel_id=1, source_target_pairs={{0,2},{1,3},{2,0},{3,1},{4,6},{5,7},{6,4},{7,5},{8,10},{9,11},{10,... | collective-permute-start | bytes 393224 | tf_op jit(solution)/shard_map/ppermute | solution.py:56
  58.6 25.5 %fusion.3 = f32[2944,256]{0,1:T(8,128)S(1)} fusion(f32[256,2048]{1,0:T(8,128)S(1)} %constant_dynamic-update-slice_fusion, f32[368,8,16,128]{3,2,1,0:T(8,128)} %bitcast.118), kind=kOutput, calls=%fused_computation.5 | convolution fusion | flops 9261023232 | bytes 29229056 | tf_op jit(solution)/shard_map/dot_general | solution.py:34
  84.8 1.1 copy.37
  85.9 1.1 copy.40
  87.0 1.2 copy.39
  88.2 1.1 copy.38
  89.3 3.2 %fusion.6 = f32[4,4,184,256]{3,2,1,0:T(8,128)S(1)} fusion(f32[1,4,184,256]{3,2,1,0:T(8,128)} %bitcast.125, f32[1,4,184,256]{3,2,1,0:T(8,128)} %bitcast.126, f32[1,4,184,256]{3,2,1,0:T(8,128)} %bitcast.127, f32[1,4,184,256]{3,2,1,0:T(8,128)} %bitcast.124), kind=kLoop, calls=%fused_computation.7 | loop fusion | flops 21102592 | bytes 6029312 | tf_op jit(solution)/shard_map/stack | solution.py:90
  92.5 1.3 dynamic-slice_bitcast_fusion
  94.2 1.4 collective-permute-start.5
  96.5 4.1 %collective-permute-start.14 = (f32[128,128]{0,1:T(8,128)S(1)}, f32[128,128]{0,1:T(8,128)S(1)}, u32[]{:S(2)}, u32[]{:S(2)}) collective-permute-start(f32[128,128]{0,1:T(8,128)S(1)} %add_add_fusion.2), channel_id=1, source_target_pairs={{0,12},{1,13},{2,14},{3,15},{4,8},{5,9},{6,10},{7,11},{8,4},{9,5},... | collective-permute-start | bytes 196616 | tf_op jit(solution)/shard_map/ppermute | solution.py:56
  102.5 3.2 %collective-permute-start.20 = (f32[128,256]{0,1:T(8,128)S(1)}, f32[128,256]{0,1:T(8,128)S(1)}, u32[]{:S(2)}, u32[]{:S(2)}) collective-permute-start(f32[128,256]{0,1:T(8,128)S(1)} %add_add_fusion.1), channel_id=1, source_target_pairs={{0,12},{1,13},{2,14},{3,15},{4,8},{5,9},{6,10},{7,11},{8,4},{9,5},... | collective-permute-start | bytes 393224 | tf_op jit(solution)/shard_map/ppermute | solution.py:56
  106.4 1.3 collective-permute-start.18
  108.0 11.7 %cholesky.44 = f32[128,128]{1,0:T(8,128)S(1)} custom-call(f32[128,128]{1,0:T(8,128)S(1)} %fusion.26), custom_call_target="Cholesky" | custom-call | tf_op jit(solution)/shard_map/jit(cholesky)/cholesky | solution.py:44
  121.1 9.8 %custom-call.6 = f32[1,128,128]{1,2,0:T(8,128)S(1)} custom-call(f32[1,128,128]{2,1,0:T(8,128)S(1)} %fusion.14), custom_call_target="InvertDiagBlocksLowerTriangular" | custom-call | tf_op jit(solution)/shard_map/jit(_solve_triangular)/triangular_solve | solution.py:45
  131.3 1.6 bitcast_add_fusion
  132.8 1.1 copy-done
  136.8 11.7 %cholesky.55 = f32[128,128]{1,0:T(8,128)S(1)} custom-call(f32[128,128]{1,0:T(8,128)S(1)} %fusion.24), custom_call_target="Cholesky" | custom-call | tf_op jit(solution)/shard_map/jit(cholesky)/cholesky | solution.py:44
  148.5 1.2 collective-permute-done.6
  150.1 2.2 %collective-permute-start.7 = (f32[2,184,256]{1,2,0:T(8,128)S(1)}, f32[2,184,256]{1,2,0:T(8,128)S(1)}, u32[]{:S(2)}, u32[]{:S(2)}) collective-permute-start(f32[2,184,256]{1,2,0:T(8,128)S(1)} %bitcast.128), channel_id=1, source_target_pairs={{0,3},{1,2},{2,1},{3,0},{4,7},{5,6},{6,5},{7,4},{8,11},{9,10},{10,... | collective-permute-start | bytes 1130504 | tf_op jit(solution)/shard_map/ppermute | solution.py:106
  153.7 9.8 %custom-call.7 = f32[1,128,128]{1,2,0:T(8,128)S(1)} custom-call(f32[1,128,128]{2,1,0:T(8,128)S(1)} %fusion.15), custom_call_target="InvertDiagBlocksLowerTriangular" | custom-call | tf_op jit(solution)/shard_map/jit(_solve_triangular)/triangular_solve | solution.py:45
  163.9 2.5 %collective-permute-start.8 = (f32[184,256]{0,1:T(8,128)S(1)}, f32[184,256]{0,1:T(8,128)S(1)}, u32[]{:S(2)}, u32[]{:S(2)}) collective-permute-start(f32[184,256]{0,1:T(8,128)S(1)} %dynamic-slice_bitcast_fusion.2), channel_id=1, source_target_pairs={{0,12},{1,13},{2,14},{3,15},{4,8},{5,9},{6,10},{7,11},{8,4},{9,5},... | collective-permute-start | bytes 565256 | tf_op jit(solution)/shard_map/ppermute | solution.py:106
  166.7 4.9 %collective-permute-done.8 = f32[184,256]{0,1:T(8,128)S(1)} collective-permute-done((f32[184,256]{0,1:T(8,128)S(1)}, f32[184,256]{0,1:T(8,128)S(1)}, u32[]{:S(2)}, u32[]{:S(2)}) %collective-permute-start.8) | collective-permute-done | bytes 188448 | tf_op jit(solution)/shard_map/ppermute | solution.py:106
  (115 shorter events, 26.8 us)
Async XLA Ops:
  3.8 0.7 collective-permute-start
  5.6 3.7 %collective-permute-start.2 = (f32[2056,128]{1,0:T(8,128)}, f32[2056,128]{1,0:T(8,128)S(1)}, u32[]{:S(2)}, u32[]{:S(2)}) collective-permute-start(f32[2056,128]{1,0:T(8,128)} %broadcast_select_fusion.1), channel_id=1, source_target_pairs={{16,48},{0,96},{17,49},{1,97},{18,50},{2,98},{19,51},{3,99},{20,52... | collective-permute-start | bytes 3158024 | tf_op jit(solution)/shard_map/ppermute | solution.py:70
  6.3 30.9 %collective-permute-start.1 = (f32[2056,128]{1,0:T(8,128)S(1)}, f32[2056,128]{1,0:T(8,128)}, u32[]{:S(2)}, u32[]{:S(2)}) collective-permute-start(f32[2056,128]{1,0:T(8,128)S(1)} %collective-permute-done), channel_id=1, source_target_pairs={{32,64},{112,80},{33,65},{113,81},{34,66},{114,82},{35,67},{115,83... | collective-permute-start | bytes 3158024 | tf_op jit(solution)/shard_map/ppermute | solution.py:69
  7.6 34.7 %collective-permute-start.3 = (f32[2056,128]{1,0:T(8,128)}, f32[2056,128]{1,0:T(8,128)}, u32[]{:S(2)}, u32[]{:S(2)}) collective-permute-start(f32[2056,128]{1,0:T(8,128)} %pad_maximum_fusion), channel_id=1, source_target_pairs={{0,16},{16,0},{1,17},{17,1},{2,18},{18,2},{3,19},{19,3},{4,20},{20... | collective-permute-start | bytes 3158024 | tf_op jit(solution)/shard_map/ppermute | solution.py:67
  9.2 31.6 %copy-start.3 = (s32[23,1,128]{2,1,0:T(1,128)S(1)}, s32[23,1,128]{2,1,0:T(1,128)}, u32[]{:S(2)}) copy-start(s32[23,1,128]{2,1,0:T(1,128)} %param.13) | copy-start | bytes 35332
  9.2 31.7 %copy-start.4 = (f32[23,1,128]{2,1,0:T(1,128)S(1)}, f32[23,1,128]{2,1,0:T(1,128)}, u32[]{:S(2)}) copy-start(f32[23,1,128]{2,1,0:T(1,128)} %param.14) | copy-start | bytes 35332
  38.8 4.6 %collective-permute-start.4 = (f32[2056,128]{1,0:T(8,128)S(1)}, f32[2056,128]{1,0:T(8,128)S(1)}, u32[]{:S(2)}, u32[]{:S(2)}) collective-permute-start(f32[2056,128]{1,0:T(8,128)S(1)} %select_select_fusion), channel_id=1, source_target_pairs={{32,48},{48,32},{64,80},{80,64},{96,112},{112,96},{33,49},{49,33},... | collective-permute-start | bytes 3158024 | tf_op jit(solution)/shard_map/ppermute | solution.py:78
  47.1 46.7 %collective-permute-start.10 = (f32[128,128]{0,1:T(8,128)S(1)}, f32[128,128]{0,1:T(8,128)S(1)}, u32[]{:S(2)}, u32[]{:S(2)}) collective-permute-start(f32[128,128]{0,1:T(8,128)S(1)} %fusion.62), channel_id=1, source_target_pairs={{0,2},{1,3},{2,0},{3,1},{4,6},{5,7},{6,4},{7,5},{8,10},{9,11},{10,... | collective-permute-start | bytes 196616 | tf_op jit(solution)/shard_map/ppermute | solution.py:56
  50.4 43.8 %collective-permute-start.9 = (f32[128,128]{0,1:T(8,128)S(1)}, f32[128,128]{0,1:T(8,128)}, u32[]{:S(2)}, u32[]{:S(2)}) collective-permute-start(f32[128,128]{0,1:T(8,128)S(1)} %fusion.62), channel_id=1, source_target_pairs={{0,1},{1,0},{2,3},{3,2},{4,5},{5,4},{6,7},{7,6},{8,9},{9,8},{10,11... | collective-permute-start | bytes 196616 | tf_op jit(solution)/shard_map/ppermute | solution.py:56
  51.0 44.6 %collective-permute-start.11 = (f32[128,128]{0,1:T(8,128)S(1)}, f32[128,128]{0,1:T(8,128)}, u32[]{:S(2)}, u32[]{:S(2)}) collective-permute-start(f32[128,128]{0,1:T(8,128)S(1)} %fusion.62), channel_id=1, source_target_pairs={{0,3},{1,2},{2,1},{3,0},{4,7},{5,6},{6,5},{7,4},{8,11},{9,10},{10,... | collective-permute-start | bytes 196616 | tf_op jit(solution)/shard_map/ppermute | solution.py:56
  54.8 45.8 %collective-permute-start.16 = (f32[128,256]{0,1:T(8,128)S(1)}, f32[128,256]{0,1:T(8,128)S(1)}, u32[]{:S(2)}, u32[]{:S(2)}) collective-permute-start(f32[128,256]{0,1:T(8,128)S(1)} %fusion.64), channel_id=1, source_target_pairs={{0,2},{1,3},{2,0},{3,1},{4,6},{5,7},{6,4},{7,5},{8,10},{9,11},{10,... | collective-permute-start | bytes 393224 | tf_op jit(solution)/shard_map/ppermute | solution.py:56
  57.9 42.7 %collective-permute-start.15 = (f32[128,256]{0,1:T(8,128)S(1)}, f32[128,256]{0,1:T(8,128)}, u32[]{:S(2)}, u32[]{:S(2)}) collective-permute-start(f32[128,256]{0,1:T(8,128)S(1)} %fusion.64), channel_id=1, source_target_pairs={{0,1},{1,0},{2,3},{3,2},{4,5},{5,4},{6,7},{7,6},{8,9},{9,8},{10,11... | collective-permute-start | bytes 393224 | tf_op jit(solution)/shard_map/ppermute | solution.py:56
  92.5 15.2 %copy-start.8 = (f32[128]{0:T(128)S(1)}, f32[128]{0:T(128)}, u32[]{:S(2)}) copy-start(f32[128]{0:T(128)} %get-tuple-element.55) | copy-start | bytes 1540
  93.8 7.8 %collective-permute-start.17 = (f32[128,256]{0,1:T(8,128)S(1)}, f32[128,256]{0,1:T(8,128)S(1)}, u32[]{:S(2)}, u32[]{:S(2)}) collective-permute-start(f32[128,256]{0,1:T(8,128)S(1)} %fusion.64), channel_id=1, source_target_pairs={{0,3},{1,2},{2,1},{3,0},{4,7},{5,6},{6,5},{7,4},{8,11},{9,10},{10,... | collective-permute-start | bytes 393224 | tf_op jit(solution)/shard_map/ppermute | solution.py:56
  94.2 37.1 %collective-permute-start.5 = (f32[2,2,2,184,256]{4,3,2,1,0:T(8,128)}, f32[2,2,2,184,256]{4,3,2,1,0:T(8,128)}, u32[]{:S(2)}, u32[]{:S(2)}) collective-permute-start(f32[2,2,2,184,256]{4,3,2,1,0:T(8,128)} %dynamic-slice_bitcast_fusion), channel_id=1, source_target_pairs={{0,1},{1,0},{2,3},{3,2},{4,5},{5,4},{6,7},{7,6},{8,9},{9,8},{10,11... | collective-permute-start | bytes 4521992 | tf_op jit(solution)/shard_map/ppermute | solution.py:106
  96.5 9.3 %collective-permute-start.14 = (f32[128,128]{0,1:T(8,128)S(1)}, f32[128,128]{0,1:T(8,128)S(1)}, u32[]{:S(2)}, u32[]{:S(2)}) collective-permute-start(f32[128,128]{0,1:T(8,128)S(1)} %add_add_fusion.2), channel_id=1, source_target_pairs={{0,12},{1,13},{2,14},{3,15},{4,8},{5,9},{6,10},{7,11},{8,4},{9,5},... | collective-permute-start | bytes 196616 | tf_op jit(solution)/shard_map/ppermute | solution.py:56
  100.6 5.8 %collective-permute-start.13 = (f32[128,128]{0,1:T(8,128)S(1)}, f32[128,128]{0,1:T(8,128)S(1)}, u32[]{:S(2)}, u32[]{:S(2)}) collective-permute-start(f32[128,128]{0,1:T(8,128)S(1)} %add_add_fusion.2), channel_id=1, source_target_pairs={{0,8},{1,9},{2,10},{3,11},{4,12},{5,13},{6,14},{7,15},{8,0},{9,1},... | collective-permute-start | bytes 196616 | tf_op jit(solution)/shard_map/ppermute | solution.py:56
  100.6 7.0 %collective-permute-start.12 = (f32[128,128]{0,1:T(8,128)S(1)}, f32[128,128]{0,1:T(8,128)S(1)}, u32[]{:S(2)}, u32[]{:S(2)}) collective-permute-start(f32[128,128]{0,1:T(8,128)S(1)} %add_add_fusion.2), channel_id=1, source_target_pairs={{0,4},{1,5},{2,6},{3,7},{4,0},{5,1},{6,2},{7,3},{8,12},{9,13},{10,... | collective-permute-start | bytes 196616 | tf_op jit(solution)/shard_map/ppermute | solution.py:56
  102.5 32.4 %collective-permute-start.20 = (f32[128,256]{0,1:T(8,128)S(1)}, f32[128,256]{0,1:T(8,128)S(1)}, u32[]{:S(2)}, u32[]{:S(2)}) collective-permute-start(f32[128,256]{0,1:T(8,128)S(1)} %add_add_fusion.1), channel_id=1, source_target_pairs={{0,12},{1,13},{2,14},{3,15},{4,8},{5,9},{6,10},{7,11},{8,4},{9,5},... | collective-permute-start | bytes 393224 | tf_op jit(solution)/shard_map/ppermute | solution.py:56
  105.8 29.2 %collective-permute-start.19 = (f32[128,256]{0,1:T(8,128)S(1)}, f32[128,256]{0,1:T(8,128)}, u32[]{:S(2)}, u32[]{:S(2)}) collective-permute-start(f32[128,256]{0,1:T(8,128)S(1)} %add_add_fusion.1), channel_id=1, source_target_pairs={{0,8},{1,9},{2,10},{3,11},{4,12},{5,13},{6,14},{7,15},{8,0},{9,1},... | collective-permute-start | bytes 393224 | tf_op jit(solution)/shard_map/ppermute | solution.py:56
  106.4 28.5 %collective-permute-start.18 = (f32[128,256]{0,1:T(8,128)S(1)}, f32[128,256]{0,1:T(8,128)}, u32[]{:S(2)}, u32[]{:S(2)}) collective-permute-start(f32[128,256]{0,1:T(8,128)S(1)} %add_add_fusion.1), channel_id=1, source_target_pairs={{0,4},{1,5},{2,6},{3,7},{4,0},{5,1},{6,2},{7,3},{8,12},{9,13},{10,... | collective-permute-start | bytes 393224 | tf_op jit(solution)/shard_map/ppermute | solution.py:56
  134.0 2.4 %copy-start.15 = (f32[128]{0:T(128)S(1)}, f32[128]{0:T(128)}, u32[]{:S(2)}) copy-start(f32[128]{0:T(128)} %get-tuple-element.51) | copy-start | bytes 1540
  134.1 15.6 %copy-start.1 = (f32[2,2,2,184,256]{4,3,2,1,0:T(8,128)S(1)}, f32[2,2,2,184,256]{4,3,2,1,0:T(8,128)}, u32[]{:S(2)}) copy-start(f32[2,2,2,184,256]{4,3,2,1,0:T(8,128)} %copy-done) | copy-start | bytes 4521988
  134.1 15.6 %collective-permute-start.6 = (f32[2,2,184,256]{3,2,1,0:T(8,128)S(1)}, f32[2,2,184,256]{3,2,1,0:T(8,128)S(1)}, u32[]{:S(2)}, u32[]{:S(2)}) collective-permute-start(f32[2,2,184,256]{3,2,1,0:T(8,128)S(1)} %dynamic-slice_bitcast_fusion.1), channel_id=1, source_target_pairs={{0,4},{1,5},{2,6},{3,7},{4,0},{5,1},{6,2},{7,3},{8,12},{9,13},{10,... | collective-permute-start | bytes 2261000 | tf_op jit(solution)/shard_map/ppermute | solution.py:106
  150.0 21.6 %copy-start.5 = (f32[1,184]{1,0:T(1,128)S(1)}, f32[1,184]{1,0:T(1,128)}, u32[]{:S(2)}) copy-start(f32[1,184]{1,0:T(1,128)} %get-tuple-element.66) | copy-start | bytes 2212
  150.0 21.6 %copy-start.6 = (f32[1,184]{1,0:T(1,128)S(1)}, f32[1,184]{1,0:T(1,128)}, u32[]{:S(2)}) copy-start(f32[1,184]{1,0:T(1,128)} %get-tuple-element.67) | copy-start | bytes 2212
  150.1 13.7 %collective-permute-start.7 = (f32[2,184,256]{1,2,0:T(8,128)S(1)}, f32[2,184,256]{1,2,0:T(8,128)S(1)}, u32[]{:S(2)}, u32[]{:S(2)}) collective-permute-start(f32[2,184,256]{1,2,0:T(8,128)S(1)} %bitcast.128), channel_id=1, source_target_pairs={{0,3},{1,2},{2,1},{3,0},{4,7},{5,6},{6,5},{7,4},{8,11},{9,10},{10,... | collective-permute-start | bytes 1130504 | tf_op jit(solution)/shard_map/ppermute | solution.py:106
  163.5 8.3 %copy-start.7 = (f32[128]{0:T(128)S(1)}, f32[128]{0:T(128)}, u32[]{:S(2)}) copy-start(f32[128]{0:T(128)} %slice.224) | copy-start | bytes 1540
  163.5 8.7 %copy-start.10 = (f32[128]{0:T(128)S(1)}, f32[128]{0:T(128)}, u32[]{:S(2)}) copy-start(f32[128]{0:T(128)} %get-tuple-element.52) | copy-start | bytes 1540
  163.5 8.7 %copy-start.12 = (f32[128]{0:T(128)S(1)}, f32[128]{0:T(128)}, u32[]{:S(2)}) copy-start(f32[128]{0:T(128)} %get-tuple-element.53) | copy-start | bytes 1540
  163.5 8.7 %copy-start.14 = (f32[128]{0:T(128)S(1)}, f32[128]{0:T(128)}, u32[]{:S(2)}) copy-start(f32[128]{0:T(128)} %get-tuple-element.54) | copy-start | bytes 1540
  163.9 7.7 %collective-permute-start.8 = (f32[184,256]{0,1:T(8,128)S(1)}, f32[184,256]{0,1:T(8,128)S(1)}, u32[]{:S(2)}, u32[]{:S(2)}) collective-permute-start(f32[184,256]{0,1:T(8,128)S(1)} %dynamic-slice_bitcast_fusion.2), channel_id=1, source_target_pairs={{0,12},{1,13},{2,14},{3,15},{4,8},{5,9},{6,10},{7,11},{8,4},{9,5},... | collective-permute-start | bytes 565256 | tf_op jit(solution)/shard_map/ppermute | solution.py:106
  (5 other events, 8.0 us)
